TPU v7x, 256 devices: a whole 4x4x8 slice. The times are simulated.
256 devices in a mesh: space: 64 (over x_hi, y, z), dp: 4 (over x_lo, core).
Axes of the slice: x: 4 (x_hi: 2, x_lo: 2; x = x_hi * 2 + x_lo), y: 4, z: 8, core: 2. Of those that a mesh axis runs over, the one named last changes fastest.
Arguments:
- input_states: bfloat16 [4, 64, 200, 1024], P('dp', 'space'), may hold values from -6 to 6
- loss_sensitivity: bfloat16 [4, 64, 200, 1024], P('dp', 'space'), may hold values from -6 to 6
- ocean: int32 [64, 1024], P('space'), may hold values 0 or 1
- neighbours: int32 [64, 8], P('space'), may hold values from -1 to 63, as said below
- fold_flag: int32 [64], P('space'), may hold values from 0 to 1, as said below
- w_first: bfloat16 [9, 200, 200], replicated, may hold values from -0.125 to 0.125
- w_second: bfloat16 [9, 200, 200], replicated, may hold values from -0.125 to 0.125
Outputs:
- prediction: bfloat16 [4, 64, 200, 1024], P('dp', 'space')
- earlier_kernel_slope: float32 [9, 200, 200], replicated
- latter_kernel_slope: float32 [9, 200, 200], replicated
Inputs may be any that keep to these rules, and one draw needn't show every extreme that they name: Tiles sit on a grid of 6 x 16 tile positions, some of them land; the ocean tiles carry numbers 0 to 63 in no particular order of positions; longitude wraps; the top row's northern neighbour is the mirrored tile of the same row (fold_flag 1) and its diagonal northern neighbours are -1. The relation is symmetric: if u is t's neighbour in one direction, t is u's in the opposite one (north for north across the fold). `fold_flag`: 1 exactly for tiles of the top tile row.
All inputs are finite; a program needn't handle non-finite values. No bound on the sum of `ocean` on one device may be relied on, other than what follows from the above.
Results may differ from a plain program's by a relative error of at most 0.005.
Values may be sent and summed in bfloat16 or wider, within the bound.
No kernel may reach another device: no remote copies, remote signals or barrier semaphores. Data moves between devices by JAX's collectives and lax.ppermute only.
A program may use at most 64 MiB of HBM per device.

v0:
```python
import jax
import jax.numpy as jnp
from jax import lax
from jax.sharding import PartitionSpec as P

SIDE = 32
SQRT_TWO_PI = 0.7978845608028654
CUBIC = 0.044715


def gelu_pair(a):
    inner = SQRT_TWO_PI * (a + CUBIC * a * a * a)
    tangent = jnp.tanh(inner)
    value = 0.5 * a * (1.0 + tangent)
    slope = 0.5 * (1.0 + tangent) + 0.5 * a * (1.0 - tangent * tangent) * SQRT_TWO_PI * (
        1.0 + 3.0 * CUBIC * a * a
    )
    return (value, slope)


def edge_strips(field):
    patch_extent = field.shape[2]
    return jnp.concatenate(
        [
            field[:, :, 0, :],
            field[:, :, patch_extent - 1, :],
            field[:, :, :, 0],
            field[:, :, :, patch_extent - 1],
        ],
        axis=2,
    )


def strip_parts(piece, neighbours, fold_flag):
    amount = piece.shape[0]
    patch_extent = piece.shape[2] // 4

    def pick(k):
        index = neighbours[:, k]
        valid = ((index >= 0) & (index < amount)).astype(piece.dtype)
        return jnp.take(piece, jnp.clip(index, 0, amount - 1), axis=0) * valid[:, None, None]

    from_north = pick(0)
    north = jnp.where(
        (fold_flag == 1)[:, None, None],
        from_north[:, :, patch_extent : 2 * patch_extent][:, :, ::-1],
        from_north[:, :, 0:patch_extent],
    )
    south = pick(1)[:, :, patch_extent : 2 * patch_extent]
    east = pick(2)[:, :, 2 * patch_extent : 3 * patch_extent]
    west = pick(3)[:, :, 3 * patch_extent : 4 * patch_extent]
    corners = jnp.stack(
        [
            pick(4)[:, :, 0],
            pick(5)[:, :, patch_extent - 1],
            pick(6)[:, :, patch_extent],
            pick(7)[:, :, 2 * patch_extent - 1],
        ],
        axis=-1,
    )
    return (north, south, east, west, corners)


def collect_rims(strips, neighbours, fold_flag):
    found = strip_parts(lax.all_gather(strips, "space", axis=0, tiled=True), neighbours, fold_flag)
    return tuple((b for b in found))


def padded_tiles(field, parts):
    north, south, east, west, corners = parts
    middle = jnp.concatenate([west[..., None], field, east[..., None]], axis=3)
    bottom = jnp.concatenate([corners[:, :, 3:4], south, corners[:, :, 2:3]], axis=2)[:, :, None, :]
    top = jnp.concatenate([corners[:, :, 1:2], north, corners[:, :, 0:1]], axis=2)[:, :, None, :]
    return jnp.concatenate([bottom, middle, top], axis=2)


def window(padded, shift_r, shift_c):
    patch_extent = padded.shape[2] - 2
    part = padded[
        :, :, 1 + shift_r : 1 + shift_r + patch_extent, 1 + shift_c : 1 + shift_c + patch_extent
    ]
    return part.reshape(padded.shape[0], padded.shape[1], patch_extent * patch_extent)


def conv_forward(padded, weights):
    total = None
    for k in range(9):
        term = jnp.einsum(
            "oi,tic->toc",
            weights[k],
            window(padded, k // 3 - 1, k % 3 - 1),
            preferred_element_type=jnp.float32,
        )
        total = term if total is None else total + term
    return total


def conv_adjoint(padded, weights):
    total = None
    for k in range(9):
        term = jnp.einsum(
            "oi,toc->tic",
            weights[k],
            window(padded, 1 - k // 3, 1 - k % 3),
            preferred_element_type=jnp.float32,
        )
        total = term if total is None else total + term
    return total


def weight_grad(grads, padded):
    return jnp.stack(
        [
            jnp.einsum(
                "toc,tic->oi",
                grads,
                window(padded, k // 3 - 1, k % 3 - 1),
                preferred_element_type=jnp.float32,
            )
            for k in range(9)
        ],
        axis=0,
    )


def body(input_states, loss_sensitivity, ocean, neighbours, fold_flag, w_first, w_second):
    tiles = input_states[0]
    patch_total, feature_depth, cells = tiles.shape
    patch_extent = SIDE
    inputs = tiles.reshape(patch_total, feature_depth, patch_extent, patch_extent)
    water_indicator = ocean.astype(jnp.float32)[:, None, :]
    masked_grad = (loss_sensitivity[0].astype(jnp.float32) * water_indicator).astype(jnp.bfloat16)
    grad_tiles = masked_grad.reshape(patch_total, feature_depth, patch_extent, patch_extent)
    field_parts = collect_rims(edge_strips(inputs), neighbours, fold_flag)
    in_padded = padded_tiles(inputs, field_parts)
    pre_first = conv_forward(in_padded, w_first)
    value, slope = gelu_pair(pre_first)
    hidden = (value * water_indicator).astype(jnp.bfloat16)
    hidden_tiles = hidden.reshape(patch_total, feature_depth, patch_extent, patch_extent)
    hidden_parts = collect_rims(edge_strips(hidden_tiles), neighbours, fold_flag)
    hidden_padded = padded_tiles(hidden_tiles, hidden_parts)
    latter_linear_response = conv_forward(hidden_padded, w_second)
    prediction = (latter_linear_response * water_indicator).astype(jnp.bfloat16)[None]
    grad_parts = collect_rims(edge_strips(grad_tiles), neighbours, fold_flag)
    grad_padded = padded_tiles(grad_tiles, grad_parts)
    latter_kernel_slope = weight_grad(masked_grad, hidden_padded)
    back = conv_adjoint(grad_padded, w_second).reshape(
        patch_total, feature_depth, patch_extent, patch_extent
    )
    top_row = grad_padded[:, :, patch_extent + 1, :]
    correction = jnp.zeros((patch_total, feature_depth, patch_extent), jnp.float32)
    for shift_c in (-1, 0, 1):
        segment = top_row[:, :, 1 - shift_c : 1 - shift_c + patch_extent]
        correction = correction + jnp.einsum(
            "oi,toc->tic", w_second[7 - shift_c], segment, preferred_element_type=jnp.float32
        )
        correction = correction - jnp.einsum(
            "oi,toc->tic", w_second[1 + shift_c], segment, preferred_element_type=jnp.float32
        )
    flipped = (fold_flag == 1).astype(jnp.float32)[:, None, None]
    back = back.at[:, :, patch_extent - 1, :].add(correction * flipped)
    pre_grad = (back.reshape(patch_total, feature_depth, cells) * water_indicator * slope).astype(
        jnp.bfloat16
    )
    earlier_kernel_slope = weight_grad(pre_grad, in_padded)
    earlier_kernel_slope, latter_kernel_slope = lax.psum(
        (earlier_kernel_slope, latter_kernel_slope), ("space", "dp")
    )
    return (prediction, earlier_kernel_slope, latter_kernel_slope)


def solution(mesh):
    placed = (
        P("dp", "space", None, None),
        P("dp", "space", None, None),
        P("space", None),
        P("space", None),
        P("space"),
        P(),
        P(),
    )
    return jax.shard_map(
        body,
        mesh=mesh,
        in_specs=placed,
        out_specs=(P("dp", "space", None, None), P(), P()),
        check_vma=False,
    )
```

profile of v0, /device:TPU:2, one launch (start us, length us, event | category | flops | bytes accessed | tf_op | source)
XLA Modules:
  0.0 701.0 jit_solution(7048355584428669658)
XLA Ops:
  7.2 0.7 convert_reduce_fusion
  8.0 1.2 copy.238
  9.6 0.7 copy.239
  10.8 0.7 copy.211
  11.6 0.7 fusion.168
  28.2 109.5 %all-gather.8.cloned.1.call-done = bf16[64,200,128]{2,1,0:T(8,128)(2,1)} async-done(((bf16[1,200,128]{2,1,0:T(8,128)(2,1)}), bf16[64,200,128]{2,1,0:T(8,128)(2,1)}) %all-gather.8.cloned.1.call-update) | async-done | bytes 3276816 | tf_op jit(solution)/shard_map/all_gather | solution.py:65
  137.7 1.0 constant_dynamic-slice_fusion.2
  141.1 121.1 %all-gather.4.cloned.1.call-done = bf16[64,200,128]{2,1,0:T(8,128)(2,1)} async-done(((bf16[1,200,128]{2,1,0:T(8,128)(2,1)}), bf16[64,200,128]{2,1,0:T(8,128)(2,1)}) %all-gather.4.cloned.1.call-update) | async-done | bytes 3276816 | tf_op jit(solution)/shard_map/all_gather | solution.py:65
  262.1 1.0 constant_dynamic-slice_fusion.18
  264.7 1.3 pad_maximum_fusion.7
  266.0 0.5 pad_maximum_fusion
  266.5 1.5 fusion.163
  268.5 0.5 maximum_maximum_fusion.2
  271.5 0.5 convolution_add_fusion.4
  273.0 1.2 fusion
  274.2 1.5 copy.252
  275.9 1.2 copy.253
  277.5 0.8 copy-done.29
  282.4 1.6 fusion.34
  284.0 1.3 copy.224
  285.4 0.7 copy.225
  286.4 2.0 fusion.23
  288.4 2.1 fusion.22
  290.4 1.0 fusion.21
  291.4 1.0 fusion.20
  292.4 1.0 fusion.19
  293.4 1.0 fusion.18
  294.3 1.0 fusion.17
  295.3 1.0 fusion.16
  296.3 1.0 fusion.15
  297.2 109.5 %all-gather.6.cloned.1.call-done = bf16[64,200,128]{2,1,0:T(8,128)(2,1)} async-done(((bf16[1,200,128]{2,1,0:T(8,128)(2,1)}), bf16[64,200,128]{2,1,0:T(8,128)(2,1)}) %all-gather.6.cloned.1.call-update) | async-done | bytes 3276816 | tf_op jit(solution)/shard_map/all_gather | solution.py:65
  406.7 1.0 constant_dynamic-slice_fusion.10
  409.3 0.5 pad_maximum_fusion.5
  409.8 0.5 pad_maximum_fusion.1
  411.3 1.2 fusion.14
  413.3 1.2 fusion.13
  414.8 1.2 fusion.12
  416.0 1.2 fusion.11
  417.2 1.2 fusion.10
  418.4 1.2 fusion.9
  419.6 1.2 fusion.8
  420.8 1.2 fusion.7
  422.0 1.2 fusion.6
  423.2 1.4 convolution_add_fusion.13
  426.8 1.1 fusion.5
  427.9 262.3 %all-reduce.3.cloned.1.call-done = (f32[9,200,200]{2,1,0:T(8,128)}, f32[9,200,200]{2,1,0:T(8,128)}) async-done(((f32[9,200,200]{2,1,0:T(8,128)}, f32[9,200,200]{2,1,0:T(8,128)}), (f32[9,200,200]{2,1,0:T(8,128)}, f32[9,200,200]{2,1,0:T(8,128)})) %all-reduce.3.cloned.1.call-update) | async-done | bytes 2880016 | tf_op jit(solution)/shard_map/psum | solution.py:166
  690.2 3.0 copy.333
  693.2 1.2 copy.334
  (209 shorter events, 19.0 us)
Async XLA Ops:
  7.2 3.2 copy-start.13
  7.2 130.6 %all-gather.8.cloned.1.call-start = ((), (), s32[]{:S(2)}) async-start(), calls=%async_computation.2 | async-start | bytes 3328000 | tf_op jit(solution)/shard_map/all_gather | solution.py:65
  9.2 129.5 %copy-start.2 = (bf16[1,1,200,1024]{2,3,1,0:T(8,128)(2,1)}, bf16[1,1,200,1024]{2,3,1,0:T(8,128)(2,1)S(1)}, u32[]{:S(2)}) copy-start(bf16[1,1,200,1024]{2,3,1,0:T(8,128)(2,1)S(1)} %copy.238) | copy-start | bytes 1228804
  9.3 2.3 copy-start.31
  9.3 2.3 copy-start.30
  10.4 251.8 %all-gather.4.cloned.1.call-start = ((), (), s32[]{:S(2)}) async-start(), calls=%async_computation | async-start | bytes 3328000 | tf_op jit(solution)/shard_map/all_gather | solution.py:65
  10.6 129.7 %copy-start = (bf16[9,200,200]{2,1,0:T(8,128)(2,1)S(1)}, bf16[9,200,200]{2,1,0:T(8,128)(2,1)}, u32[]{:S(2)}) copy-start(bf16[9,200,200]{2,1,0:T(8,128)(2,1)} %param.17) | copy-start | bytes 2160004
  11.5 395.2 %all-gather.6.cloned.1.call-start = ((), (), s32[]{:S(2)}) async-start(), calls=%async_computation.1 | async-start | bytes 3328000 | tf_op jit(solution)/shard_map/all_gather | solution.py:65
  270.4 1.0 copy-start.3
  277.1 1.2 copy-start.29
  277.5 1.1 copy-start.12
  277.5 1.5 copy-start.11
  277.5 1.5 copy-start.9
  278.6 1.0 copy-start.1
  279.0 1.0 copy-start.14
  280.0 1.0 copy-start.7
  280.3 1.1 copy-start.5
  281.1 1.1 copy-start.23
  281.1 1.3 copy-start.28
  284.0 6.4 copy-start.10
  286.2 404.1 %all-reduce.3.cloned.1.call-start = ((), (), s32[]{:S(2)}) async-start(), calls=%async_computation.3 | async-start | bytes 7372800 | tf_op jit(solution)/shard_map/psum | solution.py:166
  288.4 4.0 copy-start.15
  291.4 2.9 copy-start.8
  292.4 2.9 copy-start.6
  293.4 2.9 copy-start.24
  409.8 6.2 copy-start.16
  410.3 1.0 copy-start.4
  412.9 6.7 copy-start.21
  412.9 7.9 %copy-start.19 = (bf16[1,200,32,32]{1,3,2,0:T(8,128)(2,1)}, bf16[1,200,32,32]{1,3,2,0:T(8,128)(2,1)S(1)}, u32[]{:S(2)}) copy-start(bf16[1,200,32,32]{1,3,2,0:T(8,128)(2,1)S(1)} %get-tuple-element.62) | copy-start | bytes 1228804
  412.9 9.1 %copy-start.17 = (bf16[1,200,32,32]{1,3,2,0:T(8,128)(2,1)}, bf16[1,200,32,32]{1,3,2,0:T(8,128)(2,1)S(1)}, u32[]{:S(2)}) copy-start(bf16[1,200,32,32]{1,3,2,0:T(8,128)(2,1)S(1)} %get-tuple-element.61) | copy-start | bytes 1228804
  414.8 2.4 copy-start.26
  423.2 1.4 copy-start.27
  424.7 1.0 copy-start.22
  425.0 1.1 copy-start.20
  425.7 1.1 copy-start.18
  690.2 3.0 copy-start.25
Sparse Core Ops, SparseCore 0:
  12.0 125.6 all-gather.7
  141.8 120.3 all-gather.3
  286.3 120.4 all-gather.5
  423.4 266.8 all-reduce.2
where the time goes:
time: 702 us; the launch traced here: 701 us
  waiting for transfers between devices  602 us (86%)
  matrix products  35.5 us (5%)
  between operations  30.7 us (4%)
  local copies, waits for them, and re-layouts  26.9 us (4%)
    all_gather x3, waiting for transfers between devices, collect_rims(): lax.all_gather(strips, 'space', axis=0, tiled=True)  340 us
    psum x1, waiting for transfers between devices, body(): lax.psum((earlier_kernel_slope, latter_kernel_slope), ('space', 'dp'))  262 us
    dot_general x18, matrix products, weight_grad(): jnp.einsum('toc,tic->oi', grads, window(padded, k // 3 - 1, k % 3 - 1), p...  21.6 us
  transfers between devices with their start and end apart: 4, of which 4 were waited for; matrix products, arithmetic and copies ran while one was open for 3% of the time, Pallas kernels for 0%

commit v1 on v0

--- a/solution.py
+++ b/solution.py
@@ -62,7 +62,10 @@
 
 
 def collect_rims(strips, neighbours, fold_flag):
-    found = strip_parts(lax.all_gather(strips, "space", axis=0, tiled=True), neighbours, fold_flag)
+    _obtain_cube = lambda matrix, in_dim: jnp.concatenate(
+        lax.all_to_all(jnp.stack(lax.axis_size("space") * [matrix]), "space", 0, 0), in_dim
+    )
+    found = strip_parts(_obtain_cube(strips, 0), neighbours, fold_flag)
     return tuple((b for b in found))
 
 

time: 702 us -> 609 us (0.87)
  waiting for transfers between devices: 602 us -> 457 us
  starting transfers between devices: 0.35 us -> 28.7 us
  local copies, waits for them, and re-layouts: 26.9 us -> 45.7 us
    all_gather x3 -> x0, waiting for transfers between devices: 340 us -> none  [collect_rims(): lax.all_gather(strips, 'space', axis=0, tiled=True)]
    all_to_all x0 -> x3, waiting for transfers between devices: none -> 195 us  [collect_rims(): lax.all_to_all(jnp.stack(lax.axis_size('space') * [matrix]), 'space', 0, 0)]
    all_to_all x0 -> x3, starting transfers between devices: none -> 28.6 us  [collect_rims(): lax.all_to_all(jnp.stack(lax.axis_size('space') * [matrix]), 'space', 0, 0)]
    all_to_all x0 -> x3, local copies, waits for them, and re-layouts: none -> 16.1 us  [collect_rims(): lax.all_to_all(jnp.stack(lax.axis_size('space') * [matrix]), 'space', 0, 0)]
  transfers between devices with their start and end apart: 4 -> 4, of which waited for: 4 -> 4; matrix products, arithmetic and copies ran while one was open for 3% -> 4% of each run, Pallas kernels for 0% -> 0%
where the time goes in v1:
time: 609 us; the launch traced here: 607 us
  waiting for transfers between devices  457 us (75%)
  local copies, waits for them, and re-layouts  45.7 us (8%)
  matrix products  35.9 us (6%)
  between operations  30.7 us (5%)
  starting transfers between devices  28.7 us (5%)
  other arithmetic  9.15 us (2%)
    psum x1, waiting for transfers between devices, body(): lax.psum((earlier_kernel_slope, latter_kernel_slope), ('space', 'dp'))  262 us
    all_to_all x3, waiting for transfers between devices, collect_rims(): lax.all_to_all(jnp.stack(lax.axis_size('space') * [matrix]), 'space', 0, 0)  195 us
    all_to_all x3, starting transfers between devices, collect_rims(): lax.all_to_all(jnp.stack(lax.axis_size('space') * [matrix]), 'space', 0, 0)  28.6 us
    dot_general x18, matrix products, weight_grad(): jnp.einsum('toc,tic->oi', grads, window(padded, k // 3 - 1, k % 3 - 1), p...  21.7 us
    all_to_all x3, local copies, waits for them, and re-layouts, collect_rims(): lax.all_to_all(jnp.stack(lax.axis_size('space') * [matrix]), 'space', 0, 0)  16.1 us
    unnamed x70, local copies, waits for them, and re-layouts  12.3 us
  transfers between devices with their start and end apart: 4, of which 4 were waited for; matrix products, arithmetic and copies ran while one was open for 4% of the time, Pallas kernels for 0%

profile of v1, /device:TPU:2, one launch (start us, length us, event | category | flops | bytes accessed | tf_op | source)
XLA Modules:
  0.0 606.9 jit_solution(6803219766860741295)
XLA Ops:
  7.2 1.2 copy.84
  8.6 2.1 stack.46
  10.7 13.8 %all-to-all-start = ((bf16[64,1,200,128]{3,2,1,0:T(8,128)(2,1)}), bf16[64,1,200,128]{3,2,1,0:T(8,128)(2,1)S(1)}, u32[]{:S(2)}, u32[]{:S(2)}) async-start(bf16[64,1,200,128]{3,2,1,0:T(8,128)(2,1)} %stack.46), calls=%async_computation | async-start | bytes 6553600 | tf_op jit(solution)/shard_map/all_to_all | solution.py:66
  24.6 2.0 copy.98
  26.7 1.2 multiply_convert_fusion.1
  28.8 72.9 %all-to-all-done = bf16[64,1,200,128]{3,2,1,0:T(8,128)(2,1)S(1)} async-done(((bf16[64,1,200,128]{3,2,1,0:T(8,128)(2,1)}), bf16[64,1,200,128]{3,2,1,0:T(8,128)(2,1)S(1)}, u32[]{:S(2)}, u32[]{:S(2)}) %all-to-all-start) | async-done | bytes 3276832 | tf_op jit(solution)/shard_map/all_to_all | solution.py:66
  101.7 2.1 stack.48
  103.9 7.5 %all-to-all-start.2 = ((bf16[64,1,200,128]{3,2,1,0:T(8,128)(2,1)}), bf16[64,1,200,128]{3,2,1,0:T(8,128)(2,1)}, u32[]{:S(2)}, u32[]{:S(2)}) async-start(bf16[64,1,200,128]{3,2,1,0:T(8,128)(2,1)} %stack.48), calls=%async_computation.2 | async-start | bytes 6553600 | tf_op jit(solution)/shard_map/all_to_all | solution.py:66
  128.1 4.2 copy.86
  132.3 55.9 %all-to-all-done.2 = bf16[64,1,200,128]{3,2,1,0:T(8,128)(2,1)} async-done(((bf16[64,1,200,128]{3,2,1,0:T(8,128)(2,1)}), bf16[64,1,200,128]{3,2,1,0:T(8,128)(2,1)}, u32[]{:S(2)}, u32[]{:S(2)}) %all-to-all-start.2) | async-done | bytes 3276832 | tf_op jit(solution)/shard_map/all_to_all | solution.py:66
  188.2 6.0 copy.100
  194.2 0.9 select_multiply_fusion
  195.3 0.8 fusion.121
  198.9 1.5 fusion.172
  205.4 1.2 fusion
  206.6 2.5 copy.105
  209.0 1.5 fusion.27
  210.6 2.4 copy.106
  213.4 0.8 copy-done.27
  218.3 1.6 fusion.34
  219.9 1.2 copy.91
  221.3 2.1 stack.47
  223.4 7.3 %all-to-all-start.1 = ((bf16[64,1,200,128]{3,2,1,0:T(8,128)(2,1)}), bf16[64,1,200,128]{3,2,1,0:T(8,128)(2,1)}, u32[]{:S(2)}, u32[]{:S(2)}) async-start(bf16[64,1,200,128]{3,2,1,0:T(8,128)(2,1)} %stack.47), calls=%async_computation.1 | async-start | bytes 6553600 | tf_op jit(solution)/shard_map/all_to_all | solution.py:66
  230.8 2.1 fusion.23
  232.8 2.1 fusion.22
  234.9 1.0 fusion.21
  235.9 1.0 fusion.20
  236.8 1.0 fusion.19
  237.8 1.0 fusion.18
  238.8 1.0 fusion.17
  239.8 1.0 fusion.16
  240.7 1.0 fusion.15
  241.7 65.8 %all-to-all-done.1 = bf16[64,1,200,128]{3,2,1,0:T(8,128)(2,1)} async-done(((bf16[64,1,200,128]{3,2,1,0:T(8,128)(2,1)}), bf16[64,1,200,128]{3,2,1,0:T(8,128)(2,1)}, u32[]{:S(2)}, u32[]{:S(2)}) %all-to-all-start.1) | async-done | bytes 3276832 | tf_op jit(solution)/shard_map/all_to_all | solution.py:66
  307.5 5.9 copy.93
  315.0 0.9 select_multiply_fusion.1
  318.0 1.2 fusion.14
  320.0 1.2 fusion.13
  321.5 1.2 fusion.12
  322.7 1.2 fusion.11
  323.9 1.2 fusion.10
  325.1 1.2 fusion.9
  326.3 1.2 fusion.8
  327.5 1.2 fusion.7
  328.7 1.2 fusion.6
  332.7 1.1 fusion.5
  333.7 262.0 %all-reduce.3.cloned.1.call-done = (f32[9,200,200]{2,1,0:T(8,128)}, f32[9,200,200]{2,1,0:T(8,128)}) async-done(((f32[9,200,200]{2,1,0:T(8,128)}, f32[9,200,200]{2,1,0:T(8,128)}), (f32[9,200,200]{2,1,0:T(8,128)}, f32[9,200,200]{2,1,0:T(8,128)})) %all-reduce.3.cloned.1.call-update) | async-done | bytes 2880016 | tf_op jit(solution)/shard_map/psum | solution.py:169
  595.8 3.0 copy.145
  598.8 1.2 copy.146
  (147 shorter events, 21.5 us)
Async XLA Ops:
  8.4 2.3 copy-start.1
  10.7 13.8 %copy-start.29 = (s32[1,1024]{1,0:T(1,128)S(1)}, s32[1,1024]{1,0:T(1,128)}, u32[]{:S(2)}) copy-start(s32[1,1024]{1,0:T(1,128)} %param.13) | copy-start | bytes 12292
  10.7 91.0 %all-to-all-start = ((bf16[64,1,200,128]{3,2,1,0:T(8,128)(2,1)}), bf16[64,1,200,128]{3,2,1,0:T(8,128)(2,1)S(1)}, u32[]{:S(2)}, u32[]{:S(2)}) async-start(bf16[64,1,200,128]{3,2,1,0:T(8,128)(2,1)} %stack.46), calls=%async_computation | async-start | bytes 6553600 | tf_op jit(solution)/shard_map/all_to_all | solution.py:66
  27.9 0.8 copy-start.3
  103.9 7.6 %copy-start.28 = (s32[1,8]{1,0:T(1,128)S(1)}, s32[1,8]{1,0:T(1,128)}, u32[]{:S(2)}) copy-start(s32[1,8]{1,0:T(1,128)} %param.14) | copy-start | bytes 100
  103.9 84.3 %all-to-all-start.2 = ((bf16[64,1,200,128]{3,2,1,0:T(8,128)(2,1)}), bf16[64,1,200,128]{3,2,1,0:T(8,128)(2,1)}, u32[]{:S(2)}, u32[]{:S(2)}) async-start(bf16[64,1,200,128]{3,2,1,0:T(8,128)(2,1)} %stack.48), calls=%async_computation.2 | async-start | bytes 6553600 | tf_op jit(solution)/shard_map/all_to_all | solution.py:66
  132.3 64.9 %copy-start = (bf16[9,200,200]{2,1,0:T(8,128)(2,1)S(1)}, bf16[9,200,200]{2,1,0:T(8,128)(2,1)}, u32[]{:S(2)}) copy-start(bf16[9,200,200]{2,1,0:T(8,128)(2,1)} %param.17) | copy-start | bytes 2160004
  194.2 3.7 copy-start.2
  198.9 1.6 copy-start.4
  202.8 1.0 copy-start.5
  213.0 1.2 copy-start.27
  213.4 1.5 copy-start.13
  213.4 1.5 copy-start.14
  213.4 1.5 copy-start.11
  214.9 1.0 copy-start.15
  215.9 1.0 copy-start.9
  216.2 1.1 copy-start.7
  216.9 1.1 copy-start.21
  216.9 1.3 copy-start.26
  223.4 84.1 %all-to-all-start.1 = ((bf16[64,1,200,128]{3,2,1,0:T(8,128)(2,1)}), bf16[64,1,200,128]{3,2,1,0:T(8,128)(2,1)}, u32[]{:S(2)}, u32[]{:S(2)}) async-start(bf16[64,1,200,128]{3,2,1,0:T(8,128)(2,1)} %stack.47), calls=%async_computation.1 | async-start | bytes 6553600 | tf_op jit(solution)/shard_map/all_to_all | solution.py:66
  230.7 365.1 %all-reduce.3.cloned.1.call-start = ((), (), s32[]{:S(2)}) async-start(), calls=%async_computation.3 | async-start | bytes 7372800 | tf_op jit(solution)/shard_map/psum | solution.py:169
  230.8 4.1 copy-start.12
  232.8 4.0 copy-start.16
  235.9 2.9 copy-start.10
  236.8 2.9 copy-start.8
  237.8 2.9 copy-start.22
  317.0 1.0 copy-start.6
  319.6 6.7 %copy-start.19 = (bf16[1,200,32,32]{1,3,2,0:T(8,128)(2,1)}, bf16[1,200,32,32]{1,3,2,0:T(8,128)(2,1)S(1)}, u32[]{:S(2)}) copy-start(bf16[1,200,32,32]{1,3,2,0:T(8,128)(2,1)S(1)} %get-tuple-element.60) | copy-start | bytes 1228804
  319.6 7.9 %copy-start.17 = (bf16[1,200,32,32]{1,3,2,0:T(8,128)(2,1)}, bf16[1,200,32,32]{1,3,2,0:T(8,128)(2,1)S(1)}, u32[]{:S(2)}) copy-start(bf16[1,200,32,32]{1,3,2,0:T(8,128)(2,1)S(1)} %get-tuple-element.59) | copy-start | bytes 1228804
  321.5 2.4 copy-start.24
  329.9 1.0 copy-start.25
  330.9 1.0 copy-start.20
  331.2 1.1 copy-start.18
  595.8 3.0 copy-start.23
Sparse Core Ops, SparseCore 0:
  330.0 265.7 all-reduce.2
